TPU v7x, 256 devices: a whole 4x4x8 slice. The times are simulated.
256 devices in a mesh: grp: 8 (over y_hi, x), dom: 32 (over y_lo, z, core).
Axes of the slice: x: 4, y: 4 (y_hi: 2, y_lo: 2; y = y_hi * 2 + y_lo), z: 8, core: 2. Of those that a mesh axis runs over, the one named last changes fastest.
Arguments:
- fine_matrix_blocks: bfloat16 [16384, 64, 768], P(('grp', 'dom')), may hold values from -0.21875 to 0.21875
- prolongator: bfloat16 [16384, 64, 64], P(('grp', 'dom')), may hold values from -1.5 to 1.5
- block_columns: int32 [16384, 12], P(('grp', 'dom')), may hold values from 0 to 16383, as said below
- block_aggregates: int32 [16384, 12], P(('grp', 'dom')), may hold values from 0 to 1023, as said below
- live_counts: int32 [256], P(('grp', 'dom')), may hold values from 16 to 64, as said below
Outputs:
- coarse_operator: float32 [1024, 64, 768], P('dom')
Inputs may be any that keep to these rules, and one draw needn't show every extreme that they name: live_counts[p] counts the first slots of partition p that hold block rows; some partition has 64 and some has 16. `block_columns`: entry 0 of row i is i itself. For a live row of partition p, every entry is a live row of partition p - 1, p or p + 1 (only partitions that exist); entries may repeat, and repeated blocks add. block_aggregates[i, k] is the aggregate of row block_columns[i, k]. Every row of partition p, with g = p // 32 and q = p % 32, has an aggregate from (((q + 4 * g) % 32) * 8 + g) * 4 to that number plus 4 - 1.
All inputs are finite; a program needn't handle non-finite values.
Results may differ from a plain program's by a relative error of at most 0.0029.
Values may be sent and summed in bfloat16 or wider, within the bound.
No kernel may reach another device: no remote copies, remote signals or barrier semaphores. Data moves between devices by JAX's collectives and lax.ppermute only.
A program may use at most 192 MiB of HBM per device.

v0:
```python
import jax
import jax.numpy as jnp
from jax import lax
from jax.sharding import PartitionSpec as P

AGG_DEV = 4


def extended(block, sides, width):
    for axis, dim in sides:
        count = lax.axis_size(axis)
        forward = [(i, i + 1) for i in range(count - 1)]
        backward = [(target, source) for source, target in forward]
        low = lax.ppermute(
            lax.slice_in_dim(block, block.shape[dim] - width, None, axis=dim), axis, forward
        )
        high = lax.ppermute(lax.slice_in_dim(block, 0, width, axis=dim), axis, backward)
        block = jnp.concatenate([low, block, high], axis=dim)
    return block


def local(fine_matrix_blocks, prolongator, block_columns, block_aggregates, live_counts):
    capacity = fine_matrix_blocks.shape[0]
    block_width = prolongator.shape[1]
    row_blocks = block_columns.shape[1]
    slot_width = 3 * AGG_DEV
    position = lax.axis_index(("grp", "dom"))
    ghosts = extended(prolongator, ((("grp", "dom"), 0),), capacity)
    local_rows = block_columns - (position - 1) * capacity
    gathered = jnp.take(ghosts, local_rows, axis=0)
    matrix_view = fine_matrix_blocks.reshape(capacity, block_width, row_blocks, block_width)
    products = jnp.einsum(
        "ixky,ikyz->ixkz", matrix_view, gathered, preferred_element_type=jnp.float32
    )
    coarse_slot = AGG_DEV * (local_rows // capacity) + block_aggregates % AGG_DEV
    live_rows = jnp.arange(capacity) < live_counts[0]
    slot_select = (coarse_slot[:, :, None] == jnp.arange(slot_width)[None, None, :]) & live_rows[
        :, None, None
    ]
    row_sums = jnp.einsum(
        "ikt,ixkz->ixtz", slot_select.astype(jnp.float32), products, precision=lax.Precision.HIGHEST
    )
    row_sums = row_sums.astype(jnp.bfloat16).reshape(
        capacity * block_width, slot_width * block_width
    )
    row_select = (block_aggregates[:, 0:1] % AGG_DEV == jnp.arange(AGG_DEV)[None, :]) & live_rows[
        :, None
    ]
    spread = row_select.astype(jnp.bfloat16)[:, None, :, None] * prolongator[:, :, None, :]
    spread = spread.reshape(capacity * block_width, AGG_DEV * block_width)
    coarse = lax.dot_general(
        spread, row_sums, (((0,), (0,)), ((), ())), preferred_element_type=jnp.float32
    )
    groups_count = lax.axis_size("grp")
    places = lax.axis_size("dom")
    step_stride = places // groups_count
    pairs = [
        (g * places + q, g * places + (q + step_stride * g) % places)
        for g in range(groups_count)
        for q in range(places)
    ]
    rotated = lax.ppermute(coarse.astype(jnp.bfloat16), ("grp", "dom"), pairs)
    result = lax.all_gather(rotated[None], "grp", axis=0, tiled=True)
    result = result.astype(jnp.float32)
    return result.reshape(groups_count * AGG_DEV, block_width, slot_width * block_width)


def solution(mesh):
    return jax.shard_map(
        local,
        mesh=mesh,
        in_specs=(
            P(("grp", "dom"), None, None),
            P(("grp", "dom"), None, None),
            P(("grp", "dom"), None),
            P(("grp", "dom"), None),
            P(("grp", "dom")),
        ),
        out_specs=P("dom", None, None),
        check_vma=False,
    )
```

profile of v0, /device:TPU:1, one launch (start us, length us, event | category | flops | bytes accessed | tf_op | source)
XLA Modules:
  0.0 297.3 jit_solution(7769409100965928986)
XLA Ops:
  6.5 5.0 %collective-permute-start = (bf16[64,64,64]{2,1,0:T(8,128)(2,1)}, bf16[64,64,64]{2,1,0:T(8,128)(2,1)S(1)}, u32[]{:S(2)}, u32[]{:S(2)}) collective-permute-start(bf16[64,64,64]{2,1,0:T(8,128)(2,1)} %param.6), channel_id=1, source_target_pairs={{0,1},{1,2},{2,3},{3,4},{4,5},{5,6},{6,7},{7,8},{8,9},{9,10},{10,1... | collective-permute-start | bytes 1572872 | tf_op jit(solution)/shard_map/ppermute | solution.py:14
  11.6 1.9 collective-permute-start.1
  13.5 0.7 compare_and_fusion
  14.2 0.7 fusion.17
  15.0 0.7 fusion.22
  15.7 0.1 copy.14
  15.8 0.1 reshape.85
  15.9 0.1 copy.13
  16.0 19.7 %reshape.77 = bf16[64,64,12,64]{3,2,1,0:T(8,128)(2,1)} reshape(bf16[64,64,768]{2,1,0:T(8,128)(2,1)} %param.5) | data formatting | bytes 12582912 | tf_op jit(solution)/shard_map/reshape | solution.py:31
  35.7 0.1 copy.17
  36.5 0.1 copy.12
  36.6 4.2 %broadcast_multiply_fusion = bf16[64,64,4,64]{3,2,1,0:T(4,128)(2,1)} fusion(bf16[64,64,64]{2,1,0:T(8,128)(2,1)S(1)} %copy-done.1, bf16[64,4]{1,0:T(8,128)(2,1)S(1)} %copy.12), kind=kLoop, calls=%fused_computation.9 | loop fusion | flops 1048576 | bytes 2621952 | tf_op jit(solution)/shard_map/mul | solution.py:49
  40.8 7.0 %mul.38 = bf16[4096,256]{1,0:T(8,128)(2,1)} reshape(bf16[64,64,4,64]{3,2,1,0:T(4,128)(2,1)} %broadcast_multiply_fusion) | data formatting | bytes 4194304 | tf_op jit(solution)/shard_map/mul | solution.py:49
  47.8 0.0 collective-permute-done
  47.8 0.0 copy-start.2
  47.8 1.0 copy-done.2
  48.7 0.0 collective-permute-done.1
  48.7 2.2 pad_maximum_fusion
  51.0 18.2 %gather_fusion = bf16[768,64,64]{2,1,0:T(8,128)(2,1)} fusion(bf16[192,64,64]{2,1,0:T(8,128)(2,1)S(1)} %pad_maximum_fusion, s32[1024]{0:T(1024)S(1)} %pad_clamp_fusion), kind=kCustom, calls=%fused_computation | custom fusion | bytes 12585984 | tf_op jit(solution)/shard_map/jit(_take)/gather | solution.py:30
  69.1 16.6 %copy.15 = bf16[64,12,64,64]{2,3,1,0:T(8,128)(2,1)} copy(bf16[64,12,64,64]{3,2,1,0:T(8,128)(2,1)} %bitcast.19) | data formatting | bytes 12582912 | tf_op jit(solution)/shard_map/jit(_take)/gather | solution.py:30
  85.8 21.7 %fusion.4 = f32[64,64,12,64]{1,3,2,0:T(8,128)} fusion(bf16[64,64,12,64]{3,2,1,0:T(8,128)(2,1)} %reshape.77, bf16[64,12,64,64]{2,3,1,0:T(8,128)(2,1)} %copy.15, pred[64,12]{1,0:T(8,128)(4,1)S(1)} %copy.13), kind=kOutput, calls=%fused_computation.6 | convolution fusion | flops 405798912 | bytes 25166592 | tf_op jit(solution)/shard_map/ixky,ikyz->ixkz/dot_general | solution.py:32
  107.5 31.1 %copy.18 = f32[64,64,12,64]{3,2,1,0:T(8,128)} copy(f32[64,64,12,64]{1,3,2,0:T(8,128)} %fusion.4) | data formatting | bytes 25165824 | tf_op jit(solution)/shard_map/ixky,ikyz->ixkz/transpose | solution.py:32
  138.6 25.0 %convert_bitcast_fusion = bf16[64,64,12,64]{3,2,1,0:T(8,128)(2,1)} fusion(f32[64,64,12,64]{3,2,1,0:T(8,128)} %copy.18, s32[64,12]{1,0:T(8,128)S(1)} %copy.17, pred[64]{0:T(512)(128)(4,1)S(1)} %iota_compare_fusion.2), kind=kOutput, calls=%fused_computation.1 | convolution fusion | flops 456148992 | bytes 18877504 | tf_op jit(solution)/shard_map/ikt,ixkz->ixtz/dot_general | solution.py:40
  163.5 20.9 %reshape.98 = bf16[4096,768]{1,0:T(8,128)(2,1)} reshape(bf16[64,64,12,64]{3,2,1,0:T(8,128)(2,1)} %convert_bitcast_fusion) | data formatting | bytes 12582912 | tf_op jit(solution)/shard_map/reshape | solution.py:43
  184.4 4.6 %convolution_convert_fusion = bf16[256,768]{1,0:T(8,128)(2,1)S(1)} fusion(bf16[4096,256]{1,0:T(8,128)(2,1)S(1)} %copy-done, bf16[4096,768]{1,0:T(8,128)(2,1)} %reshape.98), kind=kOutput, calls=%fused_computation.10 | convolution fusion | flops 1610809344 | bytes 8781824 | tf_op jit(solution)/shard_map/dot_general | solution.py:51
  189.0 0.7 collective-permute-start.2
  189.7 0.0 collective-permute-done.2
  189.7 0.0 copy-start.3
  189.8 0.7 copy-done.3
  190.5 0.0 all-gather.3.cloned.1.call-update
  190.5 94.6 %all-gather.3.cloned.1.call-done = bf16[2048,768]{1,0:T(8,128)(2,1)} async-done(((bf16[256,768]{1,0:T(8,128)(2,1)}), bf16[2048,768]{1,0:T(8,128)(2,1)}) %all-gather.3.cloned.1.call-update) | async-done | bytes 3145744 | tf_op jit(solution)/shard_map/all_gather | solution.py:63
  285.1 5.4 %convert.1 = f32[32,64,768]{2,1,0:T(8,128)} convert(bf16[32,64,768]{2,1,0:T(8,128)(2,1)} %bitcast.20) | non-fusion elementwise | flops 1572864 | bytes 9437184 | tf_op jit(solution)/shard_map/reshape | solution.py:65
  (8 shorter events, 0.0 us)
Async XLA Ops:
  6.5 30.1 %copy-start.1 = (bf16[64,64,64]{2,1,0:T(8,128)(2,1)S(1)}, bf16[64,64,64]{2,1,0:T(8,128)(2,1)}, u32[]{:S(2)}) copy-start(bf16[64,64,64]{2,1,0:T(8,128)(2,1)} %param.6) | copy-start | bytes 1572868
  6.5 278.6 %all-gather.3.cloned.1.call-start = ((), (), s32[]{:S(2)}) async-start(), calls=%async_computation | async-start | bytes 3538944 | tf_op jit(solution)/shard_map/all_gather | solution.py:63
  6.5 41.2 %collective-permute-start = (bf16[64,64,64]{2,1,0:T(8,128)(2,1)}, bf16[64,64,64]{2,1,0:T(8,128)(2,1)S(1)}, u32[]{:S(2)}, u32[]{:S(2)}) collective-permute-start(bf16[64,64,64]{2,1,0:T(8,128)(2,1)} %param.6), channel_id=1, source_target_pairs={{0,1},{1,2},{2,3},{3,4},{4,5},{5,6},{6,7},{7,8},{8,9},{9,10},{10,1... | collective-permute-start | bytes 1572872 | tf_op jit(solution)/shard_map/ppermute | solution.py:14
  11.6 37.2 %collective-permute-start.1 = (bf16[64,64,64]{2,1,0:T(8,128)(2,1)}, bf16[64,64,64]{2,1,0:T(8,128)(2,1)}, u32[]{:S(2)}, u32[]{:S(2)}) collective-permute-start(bf16[64,64,64]{2,1,0:T(8,128)(2,1)} %param.6), channel_id=1, source_target_pairs={{1,0},{2,1},{3,2},{4,3},{5,4},{6,5},{7,6},{8,7},{9,8},{10,9},{11,1... | collective-permute-start | bytes 1572872 | tf_op jit(solution)/shard_map/ppermute | solution.py:17
  47.8 1.0 copy-start.2
  163.5 20.9 %copy-start = (bf16[4096,256]{1,0:T(8,128)(2,1)S(1)}, bf16[4096,256]{1,0:T(8,128)(2,1)}, u32[]{:S(2)}) copy-start(bf16[4096,256]{1,0:T(8,128)(2,1)} %mul.38) | copy-start | bytes 6291460
  189.0 0.7 collective-permute-start.2
  189.7 0.7 copy-start.3
Sparse Core Ops, SparseCore 0:
  190.6 94.4 all-gather.2
where the time goes:
time: 300 us; the launch traced here: 297 us
  local copies, waits for them, and re-layouts  116 us (39%)
  waiting for transfers between devices  94.6 us (32%)
  matrix products  51.3 us (17%)
  between operations  14.1 us (5%)
  other arithmetic  14 us (5%)
  starting transfers between devices  7.66 us (3%)
    all_gather x1, waiting for transfers between devices, local(): result = lax.all_gather(rotated[None], 'grp', axis=0, tiled=True)  94.6 us
    gather x2, local copies, waits for them, and re-layouts, local(): gathered = jnp.take(ghosts, local_rows, axis=0)  34.8 us
    transpose x1, local copies, waits for them, and re-layouts, local(): jnp.einsum('ixky,ikyz->ixkz', matrix_view, gathered, preferred_element_ty...  31.1 us
    dot_general x1, matrix products, local(): jnp.einsum('ikt,ixkz->ixtz', slot_select.astype(jnp.float32), products, p...  25 us
    dot_general x1, matrix products, local(): jnp.einsum('ixky,ikyz->ixkz', matrix_view, gathered, preferred_element_ty...  21.7 us
    reshape x1, local copies, waits for them, and re-layouts, local(): row_sums.astype(jnp.bfloat16)  20.9 us
    reshape x1, local copies, waits for them, and re-layouts, local(): fine_matrix_blocks.reshape(capacity, block_width, row_blocks, block_width)  19.7 us
    mul x1, local copies, waits for them, and re-layouts, local(): row_select.astype(jnp.bfloat16)[:, None, :, None]  6.95 us
  transfers between devices with their start and end apart: 4, of which 1 were waited for; matrix products, arithmetic and copies ran while one was open for 11% of the time, Pallas kernels for 0%

commit v1 on v0

--- a/solution.py
+++ b/solution.py
@@ -60,7 +60,9 @@
         for q in range(places)
     ]
     rotated = lax.ppermute(coarse.astype(jnp.bfloat16), ("grp", "dom"), pairs)
-    result = lax.all_gather(rotated[None], "grp", axis=0, tiled=True)
+    result = jnp.concatenate(
+        lax.all_to_all(jnp.stack([rotated[None]] * lax.axis_size("grp")), "grp", 0, 0), axis=0
+    )
     result = result.astype(jnp.float32)
     return result.reshape(groups_count * AGG_DEV, block_width, slot_width * block_width)
 

time: 300 us -> 260 us (0.87)
  the two profiles are of different devices: /device:TPU:1 before, /device:TPU:96 now
where the time goes in v1:
time: 260 us; the launch traced here: 257 us
  local copies, waits for them, and re-layouts  115 us (44%)
  blocking collectives  71.4 us (27%)
  matrix products  51.3 us (20%)
  other arithmetic  12.1 us (5%)
  starting transfers between devices  6.37 us (2%)
    all_to_all x1, blocking collectives, local(): lax.all_to_all(jnp.stack([rotated[None]] * lax.axis_size('grp')), 'grp',...  71.4 us
    gather x2, local copies, waits for them, and re-layouts, local(): gathered = jnp.take(ghosts, local_rows, axis=0)  34.8 us
    transpose x1, local copies, waits for them, and re-layouts, local(): jnp.einsum('ixky,ikyz->ixkz', matrix_view, gathered, preferred_element_ty...  31.1 us
    dot_general x1, matrix products, local(): jnp.einsum('ikt,ixkz->ixtz', slot_select.astype(jnp.float32), products, p...  25 us
    dot_general x1, matrix products, local(): jnp.einsum('ixky,ikyz->ixkz', matrix_view, gathered, preferred_element_ty...  21.7 us
    reshape x1, local copies, waits for them, and re-layouts, local(): row_sums.astype(jnp.bfloat16)  20.9 us
    reshape x1, local copies, waits for them, and re-layouts, local(): fine_matrix_blocks.reshape(capacity, block_width, row_blocks, block_width)  19.7 us
    mul x1, local copies, waits for them, and re-layouts, local(): row_select.astype(jnp.bfloat16)[:, None, :, None]  6.96 us
  transfers between devices with their start and end apart: 3, of which 0 were waited for; matrix products, arithmetic and copies ran while one was open for 13% of the time, Pallas kernels for 0%

profile of v1, /device:TPU:96, one launch (start us, length us, event | category | flops | bytes accessed | tf_op | source)
XLA Modules:
  0.0 257.1 jit_solution(11768309340637068309)
XLA Ops:
  0.0 2.0 collective-permute-start
  2.1 3.6 %collective-permute-start.1 = (bf16[64,64,64]{2,1,0:T(8,128)(2,1)}, bf16[64,64,64]{2,1,0:T(8,128)(2,1)}, u32[]{:S(2)}, u32[]{:S(2)}) collective-permute-start(bf16[64,64,64]{2,1,0:T(8,128)(2,1)} %param.6), channel_id=1, source_target_pairs={{1,0},{2,1},{3,2},{4,3},{5,4},{6,5},{7,6},{8,7},{9,8},{10,9},{11,1... | collective-permute-start | bytes 1572872 | tf_op jit(solution)/shard_map/ppermute | solution.py:17
  5.7 0.7 compare_and_fusion
  6.4 0.7 fusion.17
  7.1 0.7 fusion.22
  7.8 0.1 copy.21
  7.9 0.1 reshape.83
  8.0 0.1 copy.20
  8.2 19.7 %reshape.78 = bf16[64,64,12,64]{3,2,1,0:T(8,128)(2,1)} reshape(bf16[64,64,768]{2,1,0:T(8,128)(2,1)} %param.5) | data formatting | bytes 12582912 | tf_op jit(solution)/shard_map/reshape | solution.py:31
  27.9 0.1 copy.24
  28.7 0.1 copy.19
  28.8 0.0 copy-done.1
  28.8 4.2 %broadcast_multiply_fusion = bf16[64,64,4,64]{3,2,1,0:T(4,128)(2,1)} fusion(bf16[64,64,64]{2,1,0:T(8,128)(2,1)S(1)} %copy-done.1, bf16[64,4]{1,0:T(8,128)(2,1)S(1)} %copy.19), kind=kLoop, calls=%fused_computation.9 | loop fusion | flops 1048576 | bytes 2621952 | tf_op jit(solution)/shard_map/mul | solution.py:49
  33.0 7.0 %mul.38 = bf16[4096,256]{1,0:T(8,128)(2,1)} reshape(bf16[64,64,4,64]{3,2,1,0:T(4,128)(2,1)} %broadcast_multiply_fusion) | data formatting | bytes 4194304 | tf_op jit(solution)/shard_map/mul | solution.py:49
  40.0 0.0 collective-permute-done
  40.0 0.0 copy-start.2
  40.0 1.0 copy-done.2
  41.0 0.0 collective-permute-done.1
  41.0 2.2 pad_maximum_fusion
  43.2 18.2 %gather_fusion = bf16[768,64,64]{2,1,0:T(8,128)(2,1)} fusion(bf16[192,64,64]{2,1,0:T(8,128)(2,1)S(1)} %pad_maximum_fusion, s32[1024]{0:T(1024)S(1)} %pad_clamp_fusion), kind=kCustom, calls=%fused_computation | custom fusion | bytes 12585984 | tf_op jit(solution)/shard_map/jit(_take)/gather | solution.py:30
  61.4 16.6 %copy.22 = bf16[64,12,64,64]{2,3,1,0:T(8,128)(2,1)} copy(bf16[64,12,64,64]{3,2,1,0:T(8,128)(2,1)} %bitcast.19) | data formatting | bytes 12582912 | tf_op jit(solution)/shard_map/jit(_take)/gather | solution.py:30
  78.0 21.7 %fusion.4 = f32[64,64,12,64]{1,3,2,0:T(8,128)} fusion(bf16[64,64,12,64]{3,2,1,0:T(8,128)(2,1)} %reshape.78, bf16[64,12,64,64]{2,3,1,0:T(8,128)(2,1)} %copy.22, pred[64,12]{1,0:T(8,128)(4,1)S(1)} %copy.20), kind=kOutput, calls=%fused_computation.6 | convolution fusion | flops 405798912 | bytes 25166592 | tf_op jit(solution)/shard_map/ixky,ikyz->ixkz/dot_general | solution.py:32
  99.7 31.1 %copy.25 = f32[64,64,12,64]{3,2,1,0:T(8,128)} copy(f32[64,64,12,64]{1,3,2,0:T(8,128)} %fusion.4) | data formatting | bytes 25165824 | tf_op jit(solution)/shard_map/ixky,ikyz->ixkz/transpose | solution.py:32
  130.8 25.0 %convert_bitcast_fusion = bf16[64,64,12,64]{3,2,1,0:T(8,128)(2,1)} fusion(f32[64,64,12,64]{3,2,1,0:T(8,128)} %copy.25, s32[64,12]{1,0:T(8,128)S(1)} %copy.24, pred[64]{0:T(512)(128)(4,1)S(1)} %iota_compare_fusion.2), kind=kOutput, calls=%fused_computation.1 | convolution fusion | flops 456148992 | bytes 18877504 | tf_op jit(solution)/shard_map/ikt,ixkz->ixtz/dot_general | solution.py:40
  155.8 20.9 %reshape.92 = bf16[4096,768]{1,0:T(8,128)(2,1)} reshape(bf16[64,64,12,64]{3,2,1,0:T(8,128)(2,1)} %convert_bitcast_fusion) | data formatting | bytes 12582912 | tf_op jit(solution)/shard_map/reshape | solution.py:43
  176.7 0.0 copy-done
  176.7 4.6 %convolution_convert_fusion = bf16[256,768]{1,0:T(8,128)(2,1)S(1)} fusion(bf16[4096,256]{1,0:T(8,128)(2,1)S(1)} %copy-done, bf16[4096,768]{1,0:T(8,128)(2,1)} %reshape.92), kind=kOutput, calls=%fused_computation.10 | convolution fusion | flops 1610809344 | bytes 8781824 | tf_op jit(solution)/shard_map/dot_general | solution.py:51
  181.3 0.7 collective-permute-start.2
  182.0 0.0 collective-permute-done.2
  182.0 0.2 stack.3
  182.2 71.4 %all_to_all.5 = bf16[8,1,256,768]{3,2,1,0:T(8,128)(2,1)S(1)} all-to-all(bf16[8,1,256,768]{3,2,1,0:T(8,128)(2,1)S(1)} %stack.3), channel_id=1, replica_groups=mesh['grp'=8,'dom'=32] {'grp'}, dimensions={0} | all-to-all | bytes 6291456 | tf_op jit(solution)/shard_map/all_to_all | solution.py:64
  253.6 3.5 %convert.1 = f32[32,64,768]{2,1,0:T(8,128)} convert(bf16[32,64,768]{2,1,0:T(8,128)(2,1)S(1)} %bitcast.20) | non-fusion elementwise | flops 1572864 | bytes 9437184 | tf_op jit(solution)/shard_map/convert_element_type | solution.py:66
  (5 shorter events, 0.0 us)
Async XLA Ops:
  0.0 28.8 %copy-start.1 = (bf16[64,64,64]{2,1,0:T(8,128)(2,1)S(1)}, bf16[64,64,64]{2,1,0:T(8,128)(2,1)}, u32[]{:S(2)}) copy-start(bf16[64,64,64]{2,1,0:T(8,128)(2,1)} %param.6) | copy-start | bytes 1572868
  0.0 40.0 %collective-permute-start = (bf16[64,64,64]{2,1,0:T(8,128)(2,1)}, bf16[64,64,64]{2,1,0:T(8,128)(2,1)S(1)}, u32[]{:S(2)}, u32[]{:S(2)}) collective-permute-start(bf16[64,64,64]{2,1,0:T(8,128)(2,1)} %param.6), channel_id=1, source_target_pairs={{0,1},{1,2},{2,3},{3,4},{4,5},{5,6},{6,7},{7,8},{8,9},{9,10},{10,1... | collective-permute-start | bytes 1572872 | tf_op jit(solution)/shard_map/ppermute | solution.py:14
  2.1 38.9 %collective-permute-start.1 = (bf16[64,64,64]{2,1,0:T(8,128)(2,1)}, bf16[64,64,64]{2,1,0:T(8,128)(2,1)}, u32[]{:S(2)}, u32[]{:S(2)}) collective-permute-start(bf16[64,64,64]{2,1,0:T(8,128)(2,1)} %param.6), channel_id=1, source_target_pairs={{1,0},{2,1},{3,2},{4,3},{5,4},{6,5},{7,6},{8,7},{9,8},{10,9},{11,1... | collective-permute-start | bytes 1572872 | tf_op jit(solution)/shard_map/ppermute | solution.py:17
  40.0 1.0 copy-start.2
  155.8 20.9 %copy-start = (bf16[4096,256]{1,0:T(8,128)(2,1)S(1)}, bf16[4096,256]{1,0:T(8,128)(2,1)}, u32[]{:S(2)}) copy-start(bf16[4096,256]{1,0:T(8,128)(2,1)} %mul.38) | copy-start | bytes 6291460
  181.3 0.7 collective-permute-start.2
